TPU v7x, 512 devices: a whole 4x8x8 slice. The times are simulated.
512 devices in a mesh: seq: 128 (over y, z, core), tp: 4 (over x).
Axes of the slice: x: 4, y: 8, z: 8, core: 2. Of those that a mesh axis runs over, the one named last changes fastest.
Arguments:
- tokens: bfloat16 [32768, 1280], P('seq', 'tp'), may hold values from -6 to 6
- first_gain: float32 [1280], replicated, may hold values from 0.1 to 1.9
- w_query: bfloat16 [1280, 1280], P(None, 'tp')
- w_key: bfloat16 [1280, 1280], P(None, 'tp')
- w_value: bfloat16 [1280, 1280], P(None, 'tp'), may hold values from -0.15625 to 0.15625
- w_out: bfloat16 [1280, 1280], P('tp'), may hold values from -0.625 to 0.625
- segment_ids: int32 [32768], P('seq'), may hold values from 0 to 191, never falling along the last dimension, each value on 1 to 512 neighbouring positions
- keep_mask: int32 [32768], P('seq'), may hold values 0 or 1
- merge_gain: float32 [1280], replicated, may hold values from 0.1 to 1.9
- w_merge: bfloat16 [5120, 640], P('tp'), may hold values from -0.078125 to 0.078125
- merge_index: int32 [8192, 4], P('seq'), may hold values from 0 to 32767, as said below
- destination: int32 [8192], P('seq'), may hold values from 0 to 8191, as said below
Outputs:
- delivered: bfloat16 [8192, 640], P('seq', 'tp')
Inputs may be any that keep to these rules, and one draw needn't show every extreme that they name: `segment_ids`: segment numbers never fall along the tokens; each picture or clip holds 1 to 512 tokens and one holds exactly 512. `merge_index`: the four entries of merged row m are different tokens of the device that holds row m, that is of rows (m // 64) * 256 to that plus 256 - 1; every token lies in exactly one group. `destination`: a permutation of the merged rows. The owner of row m is destination[m] // 64; the 64 rows of each device go to exactly 32 owners, exactly 2 rows to each.
All inputs are finite; a program needn't handle non-finite values. No bound on the sum of `keep_mask` on one device may be relied on, other than what follows from the above.
Results may differ from a plain program's by a relative error of at most 0.022.
Values may be sent and summed in bfloat16 or wider, within the bound.
No kernel may reach another device: no remote copies, remote signals or barrier semaphores. Data moves between devices by JAX's collectives and lax.ppermute only.
A program may use at most 64 MiB of HBM per device.

v0:
```python
import jax
import jax.numpy as jnp
from jax import lax
from jax.sharding import PartitionSpec as P

HD = 80
CAP = 2
EPS = 1e-06


def from_behind(shard, axis, by):
    length = lax.axis_size(axis)
    pairs = [(i, i + by) for i in range(length) if 0 <= i + by < length]
    return lax.ppermute(shard, axis, pairs)


def layer_norm(activations, norm_gain):
    activations = activations.astype(jnp.float32)
    row_mean = jnp.mean(activations, axis=-1, keepdims=True)
    centered = activations - row_mean
    variance = jnp.mean(centered * centered, axis=-1, keepdims=True)
    return centered * lax.rsqrt(variance + EPS) * norm_gain


def body(
    tokens,
    first_gain,
    w_query,
    w_key,
    w_value,
    w_out,
    segment_ids,
    keep_mask,
    merge_gain,
    w_merge,
    merge_index,
    destination,
):
    row_count = tokens.shape[0]
    local_width = w_query.shape[1]
    heads_here = local_width // HD
    tp_size = lax.axis_size("tp")
    seq_size = lax.axis_size("seq")
    gathered = lax.all_gather(tokens, "tp", axis=1, tiled=True)
    normed = layer_norm(gathered, first_gain).astype(jnp.bfloat16)
    queries = jnp.dot(normed, w_query, preferred_element_type=jnp.float32).astype(jnp.bfloat16)
    key_rows = jnp.dot(normed, w_key, preferred_element_type=jnp.float32).astype(jnp.bfloat16)
    value_rows = jnp.dot(normed, w_value, preferred_element_type=jnp.float32).astype(jnp.bfloat16)
    paired = jnp.concatenate([key_rows, value_rows], axis=1)
    code_query = segment_ids + 1
    code_key = jnp.where(keep_mask > 0, code_query, 0)
    pair_list = [paired]
    code_list = [code_key]
    for offset in (1, 2, -1, -2):
        moved_pair, moved_code = from_behind((paired, code_key), "seq", offset)
        pair_list.append(moved_pair)
        code_list.append(moved_code)
    all_pairs = jnp.concatenate(pair_list, axis=0)
    all_codes = jnp.concatenate(code_list, axis=0)
    window = all_pairs.shape[0]
    key_heads = all_pairs[:, :local_width].reshape(window, heads_here, HD)
    value_heads = all_pairs[:, local_width:].reshape(window, heads_here, HD)
    query_heads = queries.reshape(row_count, heads_here, HD)
    score_scale = HD ** (-0.5)
    scores = (
        jnp.einsum("qhd,khd->hqk", query_heads, key_heads, preferred_element_type=jnp.float32)
        * score_scale
    )
    query_pos = jnp.arange(row_count)[:, None]
    key_pos = jnp.arange(window)[None, :]
    allowed = (code_query[:, None] == all_codes[None, :]) | (key_pos == query_pos)
    scores = jnp.where(allowed[None], scores, -1e30)
    row_max = jnp.max(scores, axis=-1, keepdims=True)
    exponent = jnp.exp(scores - row_max)
    row_total = jnp.sum(exponent, axis=-1, keepdims=True)
    weights = (exponent / row_total).astype(jnp.bfloat16)
    attended = jnp.einsum("hqk,khd->qhd", weights, value_heads, preferred_element_type=jnp.float32)
    attended = attended.reshape(row_count, local_width).astype(jnp.bfloat16)
    position = lax.axis_index("tp")
    seq_index = lax.axis_index("seq")
    local_index = merge_index - seq_index * row_count
    order = local_index.T.reshape(row_count)
    attended_sorted = jnp.take(attended, order, axis=0)
    partial_sum = jnp.dot(attended_sorted, w_out, preferred_element_type=jnp.float32)
    mixed_sum = lax.psum_scatter(
        partial_sum.astype(jnp.bfloat16), "tp", scatter_dimension=0, tiled=True
    ).astype(jnp.float32)
    column = lax.dynamic_slice_in_dim(local_index, position, 1, 1)[:, 0]
    residual = jnp.take(gathered, column, axis=0)
    updated = residual.astype(jnp.float32) + mixed_sum
    picked = layer_norm(updated, merge_gain).astype(jnp.bfloat16)
    partial_proj = jnp.dot(picked, w_merge, preferred_element_type=jnp.float32)
    projected = lax.psum_scatter(
        partial_proj.astype(jnp.bfloat16), "tp", scatter_dimension=1, tiled=True
    )
    slot_count = projected.shape[0]
    width = projected.shape[1]
    owner = destination // slot_count
    slot = destination - owner * slot_count
    lane = jnp.arange(slot_count)
    same_owner = owner[:, None] == owner[None, :]
    earlier = lane[None, :] < lane[:, None]
    rank = jnp.sum(jnp.where(same_owner & earlier, 1, 0), axis=1)
    send_pos = owner * CAP + rank
    target = jnp.arange(seq_size * CAP)
    send_hot = (send_pos[None, :] == target[:, None]).astype(jnp.bfloat16)
    send_rows = jnp.dot(send_hot, projected, preferred_element_type=jnp.float32)
    send_rows = send_rows.astype(jnp.bfloat16).reshape(seq_size, CAP, width)
    slot_code = (slot + 1).astype(jnp.float32)
    send_slot = jnp.dot(send_hot.astype(jnp.float32), slot_code, precision=lax.Precision.HIGHEST)
    slot_row = jnp.zeros((seq_size, 1, width), jnp.bfloat16)
    slot_row = slot_row.at[:, 0, :CAP].set(send_slot.reshape(seq_size, CAP).astype(jnp.bfloat16))
    send_buf = jnp.concatenate([send_rows, slot_row], axis=1).reshape(seq_size * (CAP + 1), width)
    recv = lax.all_to_all(send_buf, "seq", 0, 0, tiled=True).reshape(seq_size, CAP + 1, width)
    recv_rows = recv[:, :CAP, :].reshape(seq_size * CAP, width)
    recv_slot = recv[:, CAP, :CAP].reshape(seq_size * CAP).astype(jnp.int32) - 1
    recv_hot = (recv_slot[None, :] == lane[:, None]).astype(jnp.bfloat16)
    delivered = jnp.dot(recv_hot, recv_rows, preferred_element_type=jnp.float32)
    return delivered.astype(jnp.bfloat16)


def solution(mesh):
    return jax.shard_map(
        body,
        mesh=mesh,
        in_specs=(
            P("seq", "tp"),
            P(),
            P(None, "tp"),
            P(None, "tp"),
            P(None, "tp"),
            P("tp", None),
            P("seq"),
            P("seq"),
            P(),
            P("tp", None),
            P("seq", None),
            P("seq"),
        ),
        out_specs=P("seq", "tp"),
        check_vma=False,
    )
```

profile of v0, /device:TPU:1, one launch (start us, length us, event | category | flops | bytes accessed | tf_op | source)
XLA Modules:
  0.0 177.3 jit_solution(7128493967322918882)
XLA Ops:
  6.5 11.7 %all_gather.3 = bf16[256,1280]{0,1:T(8,128)(2,1)S(1)} all-gather(bf16[256,320]{0,1:T(8,128)(2,1)} %param.14), channel_id=1, replica_groups=mesh['seq'=128,'tp'=4] {'tp'}, dimensions={1}, use_global_device_ids=true | all-gather | bytes 819200 | tf_op jit(solution)/shard_map/all_gather | solution.py:44
  20.9 7.4 %collective-permute-start = (bf16[256,640]{0,1:T(8,128)(2,1)}, bf16[256,640]{0,1:T(8,128)(2,1)}, u32[]{:S(2)}, u32[]{:S(2)}) collective-permute-start(bf16[256,640]{0,1:T(8,128)(2,1)} %get-tuple-element.23), channel_id=1, source_target_pairs={{0,4},{4,8},{8,12},{12,16},{16,20},{20,24},{24,28},{28,32},{32,36}... | collective-permute-start | bytes 983048 | tf_op jit(solution)/shard_map/ppermute | solution.py:14
  28.4 4.0 %collective-permute-start.1 = (bf16[256,640]{0,1:T(8,128)(2,1)}, bf16[256,640]{0,1:T(8,128)(2,1)S(1)}, u32[]{:S(2)}, u32[]{:S(2)}) collective-permute-start(bf16[256,640]{0,1:T(8,128)(2,1)} %get-tuple-element.23), channel_id=1, source_target_pairs={{0,8},{4,12},{8,16},{12,20},{16,24},{20,28},{24,32},{28,36},{32,40... | collective-permute-start | bytes 983048 | tf_op jit(solution)/shard_map/ppermute | solution.py:14
  32.4 2.3 %collective-permute-start.2 = (bf16[256,640]{0,1:T(8,128)(2,1)}, bf16[256,640]{0,1:T(8,128)(2,1)S(1)}, u32[]{:S(2)}, u32[]{:S(2)}) collective-permute-start(bf16[256,640]{0,1:T(8,128)(2,1)} %get-tuple-element.23), channel_id=1, source_target_pairs={{4,0},{8,4},{12,8},{16,12},{20,16},{24,20},{28,24},{32,28},{36,32}... | collective-permute-start | bytes 983048 | tf_op jit(solution)/shard_map/ppermute | solution.py:14
  34.7 1.3 collective-permute-start.3
  36.1 3.9 %collective-permute-start.4 = (s32[256]{0:T(256)S(1)}, s32[256]{0:T(256)S(1)}, u32[]{:S(2)}, u32[]{:S(2)}) collective-permute-start(s32[256]{0:T(256)S(1)} %get-tuple-element.20), channel_id=1, source_target_pairs={{0,4},{4,8},{8,12},{12,16},{16,20},{20,24},{24,28},{28,32},{32,36}... | collective-permute-start | bytes 3080 | tf_op jit(solution)/shard_map/ppermute | solution.py:14
  40.2 2.4 %convolution_convert_fusion.1 = bf16[256,320]{0,1:T(8,128)(2,1)} fusion(bf16[1280,320]{0,1:T(8,128)(2,1)} %param.16, bf16[256,1280]{0,1:T(8,128)(2,1)S(1)} %all_gather.3, f32[1280]{0:T(1024)S(1)} %copy-done.10, f32[256]{0:T(256)S(1)} %add_rsqrt_fusion, f32[256]{0:T(256)S(1)} %broadcast_multiply_fusion), kind=kOutput, calls=%fused_computation.23 | convolution fusion | flops 211435520 | bytes 1645568 | tf_op jit(solution)/shard_map/dot_general | solution.py:46
  42.6 4.0 %collective-permute-start.5 = (s32[256]{0:T(256)S(1)}, s32[256]{0:T(256)S(1)}, u32[]{:S(2)}, u32[]{:S(2)}) collective-permute-start(s32[256]{0:T(256)S(1)} %get-tuple-element.20), channel_id=1, source_target_pairs={{0,8},{4,12},{8,16},{12,20},{16,24},{20,28},{24,32},{28,36},{32,40... | collective-permute-start | bytes 3080 | tf_op jit(solution)/shard_map/ppermute | solution.py:14
  47.3 1.9 %collective-permute-start.6 = (s32[256]{0:T(256)S(1)}, s32[256]{0:T(256)S(1)}, u32[]{:S(2)}, u32[]{:S(2)}) collective-permute-start(s32[256]{0:T(256)S(1)} %get-tuple-element.20), channel_id=1, source_target_pairs={{4,0},{8,4},{12,8},{16,12},{20,16},{24,20},{28,24},{32,28},{36,32}... | collective-permute-start | bytes 3080 | tf_op jit(solution)/shard_map/ppermute | solution.py:14
  49.2 4.0 %collective-permute-done.6 = s32[256]{0:T(256)S(1)} collective-permute-done((s32[256]{0:T(256)S(1)}, s32[256]{0:T(256)S(1)}, u32[]{:S(2)}, u32[]{:S(2)}) %collective-permute-start.6) | collective-permute-done | bytes 1056 | tf_op jit(solution)/shard_map/ppermute | solution.py:14
  53.3 1.3 collective-permute-start.7
  54.6 3.8 %collective-permute-done.7 = s32[256]{0:T(256)S(1)} collective-permute-done((s32[256]{0:T(256)S(1)}, s32[256]{0:T(256)S(1)}, u32[]{:S(2)}, u32[]{:S(2)}) %collective-permute-start.7) | collective-permute-done | bytes 1056 | tf_op jit(solution)/shard_map/ppermute | solution.py:14
  60.5 1.0 fusion.54
  61.5 2.9 %exponential_reduce_fusion = f32[4,256]{1,0:T(4,128)S(1)} fusion(pred[256,1280]{1,0:T(8,128)(4,1)S(1)} %copy-done.3, bf16[256,4,80]{0,2,1:T(8,128)(2,1)} %bitcast.38, bf16[1280,4,80]{0,2,1:T(8,128)(2,1)S(1)} %bitcast.31), kind=kOutput, calls=%fused_computation.6 | convolution fusion | flops 214959360 | bytes 1314816 | tf_op jit(solution)/shard_map/sub | solution.py:74
  64.4 4.1 %fusion.13 = bf16[4,80,256]{2,1,0:T(8,128)(2,1)} fusion(bf16[1280,4,80]{0,2,1:T(8,128)(2,1)} %bitcast.33, f32[4,256]{1,0:T(4,128)S(1)} %exponential_reduce_fusion, pred[256,1280]{1,0:T(8,128)(4,1)S(1)} %copy-done.3, bf16[256,4,80]{0,2,1:T(8,128)(2,1)} %bitcast.39, bf16[1280,4,80]{0,2,1:T(8,128)(2,1)S(1)} %bitcast.32), kind=kOutput, calls=%fused_computation.22 | convolution fusion | flops 426068224 | bytes 2297856 | tf_op jit(solution)/shard_map/hqk,khd->qhd/dot_general | solution.py:77
  68.6 1.2 copy.33
  69.7 1.2 gather_fusion.1
  70.9 1.4 convolution_convert_fusion
  73.6 34.7 %reduce-scatter.5.cloned.1.call-done = bf16[64,1280]{1,0:T(8,128)(2,1)} async-done(((bf16[256,1280]{1,0:T(8,128)(2,1)}), bf16[64,1280]{1,0:T(8,128)(2,1)}) %reduce-scatter.5.cloned.1.call-update) | async-done | bytes 163856 | tf_op jit(solution)/shard_map/reduce_scatter | solution.py:85
  108.3 1.1 fusion.18
  109.5 1.2 multiply_reduce_fusion
  110.7 1.4 convolution_convert_fusion.5
  113.3 25.1 %reduce-scatter.7.cloned.1.call-done = bf16[160,64]{1,0:T(8,128)(2,1)} async-done(((bf16[640,64]{1,0:T(8,128)(2,1)}), bf16[160,64]{1,0:T(8,128)(2,1)}) %reduce-scatter.7.cloned.1.call-update) | async-done | bytes 20496
  140.0 28.9 %all_to_all.6 = bf16[128,2,240]{2,1,0:T(2,128)(2,1)S(1)} all-to-all(bf16[128,2,240]{2,1,0:T(2,128)(2,1)S(1)} %reshape.225), channel_id=1, replica_groups=mesh['seq'=128,'tp'=4] {'seq'}, dimensions={0} | all-to-all | bytes 245760 | tf_op jit(solution)/shard_map/all_to_all | solution.py:114
  (83 shorter events, 11.3 us)
Async XLA Ops:
  6.5 104.2 %copy-start = (bf16[1280,640]{1,0:T(8,128)(2,1)S(1)}, bf16[1280,640]{1,0:T(8,128)(2,1)}, u32[]{:S(2)}) copy-start(bf16[1280,640]{1,0:T(8,128)(2,1)} %param.23) | copy-start | bytes 4915204
  6.5 12.1 %copy-start.10 = (f32[1280]{0:T(1024)S(1)}, f32[1280]{0:T(1024)}, u32[]{:S(2)}) copy-start(f32[1280]{0:T(1024)} %param.15) | copy-start | bytes 15364
  6.5 12.1 %copy-start.8 = (bf16[1280,320]{0,1:T(8,128)(2,1)S(1)}, bf16[1280,320]{0,1:T(8,128)(2,1)}, u32[]{:S(2)}) copy-start(bf16[1280,320]{0,1:T(8,128)(2,1)} %param.17) | copy-start | bytes 2457604
  6.5 101.8 %reduce-scatter.5.cloned.1.call-start = ((), (), s32[]{:S(2)}) async-start(), calls=%async_computation.3 | async-start | bytes 819200 | tf_op jit(solution)/shard_map/reduce_scatter | solution.py:85
  18.4 1.1 copy-start.9
  19.6 16.5 %copy-start.6 = (s32[256]{0:T(256)S(1)}, s32[256]{0:T(256)}, u32[]{:S(2)}) copy-start(s32[256]{0:T(256)} %param.20) | copy-start | bytes 3076
  19.6 16.5 %copy-start.7 = (s32[256]{0:T(256)S(1)}, s32[256]{0:T(256)}, u32[]{:S(2)}) copy-start(s32[256]{0:T(256)} %param.21) | copy-start | bytes 3076
  19.6 20.4 %copy-start.5 = (s32[64,4]{0,1:T(4,128)S(1)}, s32[64,4]{0,1:T(4,128)}, u32[]{:S(2)}) copy-start(s32[64,4]{0,1:T(4,128)} %param.24) | copy-start | bytes 3076
  20.9 38.4 %collective-permute-start = (bf16[256,640]{0,1:T(8,128)(2,1)}, bf16[256,640]{0,1:T(8,128)(2,1)}, u32[]{:S(2)}, u32[]{:S(2)}) collective-permute-start(bf16[256,640]{0,1:T(8,128)(2,1)} %get-tuple-element.23), channel_id=1, source_target_pairs={{0,4},{4,8},{8,12},{12,16},{16,20},{20,24},{24,28},{28,32},{32,36}... | collective-permute-start | bytes 983048 | tf_op jit(solution)/shard_map/ppermute | solution.py:14
  28.4 31.9 %collective-permute-start.1 = (bf16[256,640]{0,1:T(8,128)(2,1)}, bf16[256,640]{0,1:T(8,128)(2,1)S(1)}, u32[]{:S(2)}, u32[]{:S(2)}) collective-permute-start(bf16[256,640]{0,1:T(8,128)(2,1)} %get-tuple-element.23), channel_id=1, source_target_pairs={{0,8},{4,12},{8,16},{12,20},{16,24},{20,28},{24,32},{28,36},{32,40... | collective-permute-start | bytes 983048 | tf_op jit(solution)/shard_map/ppermute | solution.py:14
  32.4 28.0 %collective-permute-start.2 = (bf16[256,640]{0,1:T(8,128)(2,1)}, bf16[256,640]{0,1:T(8,128)(2,1)S(1)}, u32[]{:S(2)}, u32[]{:S(2)}) collective-permute-start(bf16[256,640]{0,1:T(8,128)(2,1)} %get-tuple-element.23), channel_id=1, source_target_pairs={{4,0},{8,4},{12,8},{16,12},{20,16},{24,20},{28,24},{32,28},{36,32}... | collective-permute-start | bytes 983048 | tf_op jit(solution)/shard_map/ppermute | solution.py:14
  34.7 25.7 %collective-permute-start.3 = (bf16[256,640]{0,1:T(8,128)(2,1)}, bf16[256,640]{0,1:T(8,128)(2,1)S(1)}, u32[]{:S(2)}, u32[]{:S(2)}) collective-permute-start(bf16[256,640]{0,1:T(8,128)(2,1)} %get-tuple-element.23), channel_id=1, source_target_pairs={{8,0},{12,4},{16,8},{20,12},{24,16},{28,20},{32,24},{36,28},{40,32... | collective-permute-start | bytes 983048 | tf_op jit(solution)/shard_map/ppermute | solution.py:14
  36.1 6.5 %collective-permute-start.4 = (s32[256]{0:T(256)S(1)}, s32[256]{0:T(256)S(1)}, u32[]{:S(2)}, u32[]{:S(2)}) collective-permute-start(s32[256]{0:T(256)S(1)} %get-tuple-element.20), channel_id=1, source_target_pairs={{0,4},{4,8},{8,12},{12,16},{16,20},{20,24},{24,28},{28,32},{32,36}... | collective-permute-start | bytes 3080 | tf_op jit(solution)/shard_map/ppermute | solution.py:14
  40.2 19.2 %copy-start.1 = (bf16[1280,640]{0,1:T(8,128)(2,1)S(1)}, bf16[1280,640]{0,1:T(8,128)(2,1)}, u32[]{:S(2)}) copy-start(bf16[1280,640]{0,1:T(8,128)(2,1)} %get-tuple-element.24) | copy-start | bytes 4915204
  42.6 4.7 %collective-permute-start.5 = (s32[256]{0:T(256)S(1)}, s32[256]{0:T(256)S(1)}, u32[]{:S(2)}, u32[]{:S(2)}) collective-permute-start(s32[256]{0:T(256)S(1)} %get-tuple-element.20), channel_id=1, source_target_pairs={{0,8},{4,12},{8,16},{12,20},{16,24},{20,28},{24,32},{28,36},{32,40... | collective-permute-start | bytes 3080 | tf_op jit(solution)/shard_map/ppermute | solution.py:14
  47.3 6.0 %collective-permute-start.6 = (s32[256]{0:T(256)S(1)}, s32[256]{0:T(256)S(1)}, u32[]{:S(2)}, u32[]{:S(2)}) collective-permute-start(s32[256]{0:T(256)S(1)} %get-tuple-element.20), channel_id=1, source_target_pairs={{4,0},{8,4},{12,8},{16,12},{20,16},{24,20},{28,24},{32,28},{36,32}... | collective-permute-start | bytes 3080 | tf_op jit(solution)/shard_map/ppermute | solution.py:14
  53.3 5.1 %collective-permute-start.7 = (s32[256]{0:T(256)S(1)}, s32[256]{0:T(256)S(1)}, u32[]{:S(2)}, u32[]{:S(2)}) collective-permute-start(s32[256]{0:T(256)S(1)} %get-tuple-element.20), channel_id=1, source_target_pairs={{8,0},{12,4},{16,8},{20,12},{24,16},{28,20},{32,24},{36,28},{40,32... | collective-permute-start | bytes 3080 | tf_op jit(solution)/shard_map/ppermute | solution.py:14
  60.5 1.0 copy-start.3
  68.6 2.3 %copy-start.2 = (bf16[320,1280]{1,0:T(8,128)(2,1)S(1)}, bf16[320,1280]{1,0:T(8,128)(2,1)}, u32[]{:S(2)}) copy-start(bf16[320,1280]{1,0:T(8,128)(2,1)} %param.19) | copy-start | bytes 2457604
  72.3 1.1 copy-start.11
  72.3 38.4 %copy-start.4 = (f32[1280]{0:T(1024)S(1)}, f32[1280]{0:T(1024)}, u32[]{:S(2)}) copy-start(f32[1280]{0:T(1024)} %param.22) | copy-start | bytes 15364
  72.3 66.1 %reduce-scatter.7.cloned.1.call-start = ((), (), s32[]{:S(2)}) async-start(), calls=%async_computation.4 | async-start | bytes 204800
Sparse Core Ops, SparseCore 0:
  72.4 35.8 reduce-scatter.4
  113.0 25.2 reduce-scatter.6
where the time goes:
time: 178 us; the launch traced here: 177 us
  waiting for transfers between devices  68.4 us (38%)
  blocking collectives  40.5 us (23%)
  starting transfers between devices  26.1 us (15%)
  matrix products  15.1 us (8%)
  between operations  13.8 us (8%)
  local copies, waits for them, and re-layouts  7.86 us (4%)
  other arithmetic  5.42 us (3%)
    reduce_scatter x1, waiting for transfers between devices, body(): lax.psum_scatter(partial_sum.astype(jnp.bfloat16), 'tp', scatter_dimensio...  34.7 us
    all_to_all x1, blocking collectives, body(): lax.all_to_all(send_buf, 'seq', 0, 0, tiled=True)  28.9 us
    ppermute x8, starting transfers between devices, from_behind(): return lax.ppermute(shard, axis, pairs)  26.1 us
    unnamed x3, waiting for transfers between devices  25.1 us
    all_gather x1, blocking collectives, body(): gathered = lax.all_gather(tokens, 'tp', axis=1, tiled=True)  11.7 us
    ppermute x8, waiting for transfers between devices, from_behind(): return lax.ppermute(shard, axis, pairs)  8.52 us
    dot_general x1, matrix products, body(): jnp.einsum('hqk,khd->qhd', weights, value_heads, preferred_element_type=j...  4.14 us
  transfers between devices with their start and end apart: 10, of which 5 were waited for; matrix products, arithmetic and copies ran while one was open for 4% of the time, Pallas kernels for 0%

commit v1 on v0

--- a/solution.py
+++ b/solution.py
@@ -41,7 +41,9 @@
     heads_here = local_width // HD
     tp_size = lax.axis_size("tp")
     seq_size = lax.axis_size("seq")
-    gathered = lax.all_gather(tokens, "tp", axis=1, tiled=True)
+    gathered = jnp.concatenate(
+        lax.all_to_all(jnp.stack([tokens] * lax.axis_size("tp")), "tp", 0, 0), axis=1
+    )
     normed = layer_norm(gathered, first_gain).astype(jnp.bfloat16)
     queries = jnp.dot(normed, w_query, preferred_element_type=jnp.float32).astype(jnp.bfloat16)
     key_rows = jnp.dot(normed, w_key, preferred_element_type=jnp.float32).astype(jnp.bfloat16)

time: 178 us -> 172 us (0.966)
  blocking collectives: 40.5 us -> 28.9 us
  starting transfers between devices: 26.1 us -> 29.7 us
  waiting for transfers between devices: 68.4 us -> 71.5 us
    all_gather x1 -> x0, blocking collectives: 11.7 us -> none  [body(): gathered = lax.all_gather(tokens, 'tp', axis=1, tiled=True)]
    all_to_all x0 -> x1, waiting for transfers between devices: none -> 10.2 us  [body(): lax.all_to_all(jnp.stack([tokens] * lax.axis_size('tp')), 'tp', 0, 0)]
    reduce_scatter x1, waiting for transfers between devices: 34.7 us -> 25.6 us  [body(): lax.psum_scatter(partial_sum.astype(jnp.bfloat16), 'tp', scatter_dimensio...]
    all_to_all x0 -> x1, starting transfers between devices: none -> 3.98 us  [body(): lax.all_to_all(jnp.stack([tokens] * lax.axis_size('tp')), 'tp', 0, 0)]
    ppermute x8, waiting for transfers between devices: 8.52 us -> 10.6 us  [from_behind(): return lax.ppermute(shard, axis, pairs)]
    another operation x0 -> x1, local copies, waits for them, and re-layouts: none -> 1.79 us  [body(): jnp.stack([tokens] * lax.axis_size('tp'))]
  transfers between devices with their start and end apart: 10 -> 11, of which waited for: 5 -> 6; matrix products, arithmetic and copies ran while one was open for 4% -> 3% of each run, Pallas kernels for 0% -> 0%
where the time goes in v1:
time: 172 us; the launch traced here: 171 us
  waiting for transfers between devices  71.5 us (42%)
  starting transfers between devices  29.7 us (17%)
  blocking collectives  28.9 us (17%)
  between operations  13.8 us (8%)
  matrix products  13.5 us (8%)
  local copies, waits for them, and re-layouts  8.77 us (5%)
  other arithmetic  4.9 us (3%)
    all_to_all x1, blocking collectives, body(): lax.all_to_all(send_buf, 'seq', 0, 0, tiled=True)  28.9 us
    ppermute x8, starting transfers between devices, from_behind(): return lax.ppermute(shard, axis, pairs)  25.6 us
    reduce_scatter x1, waiting for transfers between devices, body(): lax.psum_scatter(partial_sum.astype(jnp.bfloat16), 'tp', scatter_dimensio...  25.6 us
    unnamed x3, waiting for transfers between devices  25.1 us
    ppermute x8, waiting for transfers between devices, from_behind(): return lax.ppermute(shard, axis, pairs)  10.6 us
    all_to_all x1, waiting for transfers between devices, body(): lax.all_to_all(jnp.stack([tokens] * lax.axis_size('tp')), 'tp', 0, 0)  10.2 us
    dot_general x1, matrix products, body(): jnp.einsum('hqk,khd->qhd', weights, value_heads, preferred_element_type=j...  4.14 us
    all_to_all x1, starting transfers between devices, body(): lax.all_to_all(jnp.stack([tokens] * lax.axis_size('tp')), 'tp', 0, 0)  3.98 us
  transfers between devices with their start and end apart: 11, of which 6 were waited for; matrix products, arithmetic and copies ran while one was open for 3% of the time, Pallas kernels for 0%

profile of v1, /device:TPU:1, one launch (start us, length us, event | category | flops | bytes accessed | tf_op | source)
XLA Modules:
  0.0 171.0 jit_solution(2077703551842062875)
XLA Ops:
  7.4 5.5 %collective-permute-start.4 = (s32[256]{0:T(256)S(1)}, s32[256]{0:T(256)S(1)}, u32[]{:S(2)}, u32[]{:S(2)}) collective-permute-start(s32[256]{0:T(256)S(1)} %get-tuple-element.20), channel_id=1, source_target_pairs={{0,4},{4,8},{8,12},{12,16},{16,20},{20,24},{24,28},{28,32},{32,36}... | collective-permute-start | bytes 3080 | tf_op jit(solution)/shard_map/ppermute | solution.py:14
  12.9 4.0 %collective-permute-start.5 = (s32[256]{0:T(256)S(1)}, s32[256]{0:T(256)S(1)}, u32[]{:S(2)}, u32[]{:S(2)}) collective-permute-start(s32[256]{0:T(256)S(1)} %get-tuple-element.20), channel_id=1, source_target_pairs={{0,8},{4,12},{8,16},{12,20},{16,24},{20,28},{24,32},{28,36},{32,40... | collective-permute-start | bytes 3080 | tf_op jit(solution)/shard_map/ppermute | solution.py:14
  16.9 2.0 %collective-permute-start.6 = (s32[256]{0:T(256)S(1)}, s32[256]{0:T(256)S(1)}, u32[]{:S(2)}, u32[]{:S(2)}) collective-permute-start(s32[256]{0:T(256)S(1)} %get-tuple-element.20), channel_id=1, source_target_pairs={{4,0},{8,4},{12,8},{16,12},{20,16},{24,20},{28,24},{32,28},{36,32}... | collective-permute-start | bytes 3080 | tf_op jit(solution)/shard_map/ppermute | solution.py:14
  18.8 1.3 collective-permute-start.7
  20.1 1.8 %stack.2 = bf16[4,256,320]{1,2,0:T(8,128)(2,1)} broadcast(bf16[256,320]{0,1:T(8,128)(2,1)} %param.14), dimensions={1,2} | broadcast | bytes 819200 | tf_op jit(solution)/shard_map/stack | solution.py:45
  21.9 4.0 %all-to-all-start = ((bf16[4,256,320]{1,2,0:T(8,128)(2,1)}), bf16[4,256,320]{1,2,0:T(8,128)(2,1)S(1)}, u32[]{:S(2)}, u32[]{:S(2)}) async-start(bf16[4,256,320]{1,2,0:T(8,128)(2,1)} %stack.2), calls=%async_computation | async-start | bytes 1310720 | tf_op jit(solution)/shard_map/all_to_all | solution.py:45
  26.2 10.2 %all-to-all-done = bf16[4,256,320]{1,2,0:T(8,128)(2,1)S(1)} async-done(((bf16[4,256,320]{1,2,0:T(8,128)(2,1)}), bf16[4,256,320]{1,2,0:T(8,128)(2,1)S(1)}, u32[]{:S(2)}, u32[]{:S(2)}) %all-to-all-start) | async-done | bytes 655392 | tf_op jit(solution)/shard_map/all_to_all | solution.py:45
  38.4 5.9 %collective-permute-start = (bf16[256,640]{0,1:T(8,128)(2,1)S(1)}, bf16[256,640]{0,1:T(8,128)(2,1)S(1)}, u32[]{:S(2)}, u32[]{:S(2)}) collective-permute-start(bf16[256,640]{0,1:T(8,128)(2,1)S(1)} %get-tuple-element.23), channel_id=1, source_target_pairs={{0,4},{4,8},{8,12},{12,16},{16,20},{20,24},{24,28},{28,32},{32,36}... | collective-permute-start | bytes 983048 | tf_op jit(solution)/shard_map/ppermute | solution.py:14
  44.6 3.8 %collective-permute-start.1 = (bf16[256,640]{0,1:T(8,128)(2,1)S(1)}, bf16[256,640]{0,1:T(8,128)(2,1)S(1)}, u32[]{:S(2)}, u32[]{:S(2)}) collective-permute-start(bf16[256,640]{0,1:T(8,128)(2,1)S(1)} %get-tuple-element.23), channel_id=1, source_target_pairs={{0,8},{4,12},{8,16},{12,20},{16,24},{20,28},{24,32},{28,36},{32,40... | collective-permute-start | bytes 983048 | tf_op jit(solution)/shard_map/ppermute | solution.py:14
  48.4 1.9 %collective-permute-start.2 = (bf16[256,640]{0,1:T(8,128)(2,1)S(1)}, bf16[256,640]{0,1:T(8,128)(2,1)S(1)}, u32[]{:S(2)}, u32[]{:S(2)}) collective-permute-start(bf16[256,640]{0,1:T(8,128)(2,1)S(1)} %get-tuple-element.23), channel_id=1, source_target_pairs={{4,0},{8,4},{12,8},{16,12},{20,16},{24,20},{28,24},{32,28},{36,32}... | collective-permute-start | bytes 983048 | tf_op jit(solution)/shard_map/ppermute | solution.py:14
  50.3 1.3 collective-permute-start.3
  52.7 2.6 %collective-permute-done.1 = bf16[256,640]{0,1:T(8,128)(2,1)S(1)} collective-permute-done((bf16[256,640]{0,1:T(8,128)(2,1)S(1)}, bf16[256,640]{0,1:T(8,128)(2,1)S(1)}, u32[]{:S(2)}, u32[]{:S(2)}) %collective-permute-start.1) | collective-permute-done | bytes 327712 | tf_op jit(solution)/shard_map/ppermute | solution.py:14
  55.3 2.1 %collective-permute-done.2 = bf16[256,640]{0,1:T(8,128)(2,1)S(1)} collective-permute-done((bf16[256,640]{0,1:T(8,128)(2,1)S(1)}, bf16[256,640]{0,1:T(8,128)(2,1)S(1)}, u32[]{:S(2)}, u32[]{:S(2)}) %collective-permute-start.2) | collective-permute-done | bytes 327712 | tf_op jit(solution)/shard_map/ppermute | solution.py:14
  57.5 5.8 %collective-permute-done.3 = bf16[256,640]{0,1:T(8,128)(2,1)S(1)} collective-permute-done((bf16[256,640]{0,1:T(8,128)(2,1)S(1)}, bf16[256,640]{0,1:T(8,128)(2,1)S(1)}, u32[]{:S(2)}, u32[]{:S(2)}) %collective-permute-start.3) | collective-permute-done | bytes 327712 | tf_op jit(solution)/shard_map/ppermute | solution.py:14
  64.4 2.9 %exponential_reduce_fusion = f32[4,256]{1,0:T(4,128)S(1)} fusion(pred[256,1280]{1,0:T(8,128)(4,1)S(1)} %fusion.9, bf16[256,4,80]{0,2,1:T(8,128)(2,1)} %bitcast.45, bf16[1280,4,80]{0,2,1:T(8,128)(2,1)S(1)} %bitcast.41), kind=kOutput, calls=%fused_computation.6 | convolution fusion | flops 214959360 | bytes 1314816 | tf_op jit(solution)/shard_map/sub | solution.py:76
  67.3 4.1 %fusion.10 = bf16[4,80,256]{2,1,0:T(8,128)(2,1)} fusion(bf16[1280,4,80]{0,2,1:T(8,128)(2,1)} %bitcast.43, f32[4,256]{1,0:T(4,128)S(1)} %exponential_reduce_fusion, pred[256,1280]{1,0:T(8,128)(4,1)S(1)} %fusion.9, bf16[256,4,80]{0,2,1:T(8,128)(2,1)} %bitcast.46, bf16[1280,4,80]{0,2,1:T(8,128)(2,1)S(1)} %bitcast.42), kind=kOutput, calls=%fused_computation.20 | convolution fusion | flops 426068224 | bytes 2297856 | tf_op jit(solution)/shard_map/hqk,khd->qhd/dot_general | solution.py:79
  71.4 1.2 copy.33
  72.6 1.2 gather_fusion.1
  73.8 1.4 convolution_convert_fusion
  76.5 25.6 %reduce-scatter.5.cloned.1.call-done = bf16[64,1280]{1,0:T(8,128)(2,1)} async-done(((bf16[256,1280]{1,0:T(8,128)(2,1)}), bf16[64,1280]{1,0:T(8,128)(2,1)}) %reduce-scatter.5.cloned.1.call-update) | async-done | bytes 163856 | tf_op jit(solution)/shard_map/reduce_scatter | solution.py:87
  103.3 1.2 multiply_reduce_fusion
  104.5 1.4 convolution_convert_fusion.5
  107.1 25.0 %reduce-scatter.7.cloned.1.call-done = bf16[160,64]{1,0:T(8,128)(2,1)} async-done(((bf16[640,64]{1,0:T(8,128)(2,1)}), bf16[160,64]{1,0:T(8,128)(2,1)}) %reduce-scatter.7.cloned.1.call-update) | async-done | bytes 20496
  133.7 28.9 %all_to_all.11 = bf16[128,2,240]{2,1,0:T(2,128)(2,1)S(1)} all-to-all(bf16[128,2,240]{2,1,0:T(2,128)(2,1)S(1)} %reshape.240), channel_id=1, replica_groups=mesh['seq'=128,'tp'=4] {'seq'}, dimensions={0} | all-to-all | bytes 245760 | tf_op jit(solution)/shard_map/all_to_all | solution.py:116
  (80 shorter events, 12.1 us)
Async XLA Ops:
  6.5 98.0 %copy-start = (bf16[1280,640]{1,0:T(8,128)(2,1)S(1)}, bf16[1280,640]{1,0:T(8,128)(2,1)}, u32[]{:S(2)}) copy-start(bf16[1280,640]{1,0:T(8,128)(2,1)} %param.23) | copy-start | bytes 4915204
  6.5 19.4 %copy-start.7 = (s32[64,4]{0,1:T(4,128)S(1)}, s32[64,4]{0,1:T(4,128)}, u32[]{:S(2)}) copy-start(s32[64,4]{0,1:T(4,128)} %param.24) | copy-start | bytes 3076
  7.4 29.5 %copy-start.5 = (f32[1280]{0:T(1024)S(1)}, f32[1280]{0:T(1024)}, u32[]{:S(2)}) copy-start(f32[1280]{0:T(1024)} %param.15) | copy-start | bytes 15364
  7.4 18.8 %collective-permute-start.4 = (s32[256]{0:T(256)S(1)}, s32[256]{0:T(256)S(1)}, u32[]{:S(2)}, u32[]{:S(2)}) collective-permute-start(s32[256]{0:T(256)S(1)} %get-tuple-element.20), channel_id=1, source_target_pairs={{0,4},{4,8},{8,12},{12,16},{16,20},{20,24},{24,28},{28,32},{32,36}... | collective-permute-start | bytes 3080 | tf_op jit(solution)/shard_map/ppermute | solution.py:14
  12.9 13.3 %collective-permute-start.5 = (s32[256]{0:T(256)S(1)}, s32[256]{0:T(256)S(1)}, u32[]{:S(2)}, u32[]{:S(2)}) collective-permute-start(s32[256]{0:T(256)S(1)} %get-tuple-element.20), channel_id=1, source_target_pairs={{0,8},{4,12},{8,16},{12,20},{16,24},{20,28},{24,32},{28,36},{32,40... | collective-permute-start | bytes 3080 | tf_op jit(solution)/shard_map/ppermute | solution.py:14
  16.9 9.3 %collective-permute-start.6 = (s32[256]{0:T(256)S(1)}, s32[256]{0:T(256)S(1)}, u32[]{:S(2)}, u32[]{:S(2)}) collective-permute-start(s32[256]{0:T(256)S(1)} %get-tuple-element.20), channel_id=1, source_target_pairs={{4,0},{8,4},{12,8},{16,12},{20,16},{24,20},{28,24},{32,28},{36,32}... | collective-permute-start | bytes 3080 | tf_op jit(solution)/shard_map/ppermute | solution.py:14
  18.8 7.4 %collective-permute-start.7 = (s32[256]{0:T(256)S(1)}, s32[256]{0:T(256)S(1)}, u32[]{:S(2)}, u32[]{:S(2)}) collective-permute-start(s32[256]{0:T(256)S(1)} %get-tuple-element.20), channel_id=1, source_target_pairs={{8,0},{12,4},{16,8},{20,12},{24,16},{28,20},{32,24},{36,28},{40,32... | collective-permute-start | bytes 3080 | tf_op jit(solution)/shard_map/ppermute | solution.py:14
  21.9 14.4 %all-to-all-start = ((bf16[4,256,320]{1,2,0:T(8,128)(2,1)}), bf16[4,256,320]{1,2,0:T(8,128)(2,1)S(1)}, u32[]{:S(2)}, u32[]{:S(2)}) async-start(bf16[4,256,320]{1,2,0:T(8,128)(2,1)} %stack.2), calls=%async_computation | async-start | bytes 1310720 | tf_op jit(solution)/shard_map/all_to_all | solution.py:45
  25.9 11.2 %copy-start.1 = (bf16[1280,320]{0,1:T(8,128)(2,1)S(1)}, bf16[1280,320]{0,1:T(8,128)(2,1)}, u32[]{:S(2)}) copy-start(bf16[1280,320]{0,1:T(8,128)(2,1)} %param.18) | copy-start | bytes 2457604
  25.9 76.2 %reduce-scatter.5.cloned.1.call-start = ((), (), s32[]{:S(2)}) async-start(), calls=%async_computation.4 | async-start | bytes 819200 | tf_op jit(solution)/shard_map/reduce_scatter | solution.py:87
  36.8 1.1 copy-start.2
  38.0 13.6 %copy-start.3 = (bf16[1280,320]{0,1:T(8,128)(2,1)S(1)}, bf16[1280,320]{0,1:T(8,128)(2,1)}, u32[]{:S(2)}) copy-start(bf16[1280,320]{0,1:T(8,128)(2,1)} %param.16) | copy-start | bytes 2457604
  38.4 14.3 %collective-permute-start = (bf16[256,640]{0,1:T(8,128)(2,1)S(1)}, bf16[256,640]{0,1:T(8,128)(2,1)S(1)}, u32[]{:S(2)}, u32[]{:S(2)}) collective-permute-start(bf16[256,640]{0,1:T(8,128)(2,1)S(1)} %get-tuple-element.23), channel_id=1, source_target_pairs={{0,4},{4,8},{8,12},{12,16},{16,20},{20,24},{24,28},{28,32},{32,36}... | collective-permute-start | bytes 983048 | tf_op jit(solution)/shard_map/ppermute | solution.py:14
  44.6 10.8 %collective-permute-start.1 = (bf16[256,640]{0,1:T(8,128)(2,1)S(1)}, bf16[256,640]{0,1:T(8,128)(2,1)S(1)}, u32[]{:S(2)}, u32[]{:S(2)}) collective-permute-start(bf16[256,640]{0,1:T(8,128)(2,1)S(1)} %get-tuple-element.23), channel_id=1, source_target_pairs={{0,8},{4,12},{8,16},{12,20},{16,24},{20,28},{24,32},{28,36},{32,40... | collective-permute-start | bytes 983048 | tf_op jit(solution)/shard_map/ppermute | solution.py:14
  48.4 9.1 %collective-permute-start.2 = (bf16[256,640]{0,1:T(8,128)(2,1)S(1)}, bf16[256,640]{0,1:T(8,128)(2,1)S(1)}, u32[]{:S(2)}, u32[]{:S(2)}) collective-permute-start(bf16[256,640]{0,1:T(8,128)(2,1)S(1)} %get-tuple-element.23), channel_id=1, source_target_pairs={{4,0},{8,4},{12,8},{16,12},{20,16},{24,20},{28,24},{32,28},{36,32}... | collective-permute-start | bytes 983048 | tf_op jit(solution)/shard_map/ppermute | solution.py:14
  50.3 13.0 %collective-permute-start.3 = (bf16[256,640]{0,1:T(8,128)(2,1)S(1)}, bf16[256,640]{0,1:T(8,128)(2,1)S(1)}, u32[]{:S(2)}, u32[]{:S(2)}) collective-permute-start(bf16[256,640]{0,1:T(8,128)(2,1)S(1)} %get-tuple-element.23), channel_id=1, source_target_pairs={{8,0},{12,4},{16,8},{20,12},{24,16},{28,20},{32,24},{36,28},{40,32... | collective-permute-start | bytes 983048 | tf_op jit(solution)/shard_map/ppermute | solution.py:14
  71.4 2.3 %copy-start.4 = (bf16[320,1280]{1,0:T(8,128)(2,1)S(1)}, bf16[320,1280]{1,0:T(8,128)(2,1)}, u32[]{:S(2)}) copy-start(bf16[320,1280]{1,0:T(8,128)(2,1)} %param.19) | copy-start | bytes 2457604
  72.6 2.7 %copy-start.8 = (s32[64]{0:T(128)S(1)}, s32[64]{0:T(128)}, u32[]{:S(2)}) copy-start(s32[64]{0:T(128)} %param.25) | copy-start | bytes 772
  75.2 56.9 %reduce-scatter.7.cloned.1.call-start = ((), (), s32[]{:S(2)}) async-start(), calls=%async_computation.5 | async-start | bytes 204800
  75.5 29.0 %copy-start.6 = (f32[1280]{0:T(1024)S(1)}, f32[1280]{0:T(1024)}, u32[]{:S(2)}) copy-start(f32[1280]{0:T(1024)} %param.22) | copy-start | bytes 15364
Sparse Core Ops, SparseCore 0:
  75.3 26.7 reduce-scatter.4
  106.8 25.2 reduce-scatter.6
